TPU v7x, 128 devices: a whole 4x4x4 slice. The times are simulated.
128 devices in a mesh: dp: 32 (over y, x, core), mp: 4 (over z).
Axes of the slice: x: 4, y: 4, z: 4, core: 2. Of those that a mesh axis runs over, the one named last changes fastest.
Arguments:
- hidden: bfloat16 [4096, 2560], P('dp', 'mp'), may hold values from -6 to 6
- norm_gain: bfloat16 [2560], replicated, may hold values from 0.5 to 1.5
- shared_gate: bfloat16 [2560, 3072], P(None, 'mp'), may hold values from -0.125 to 0.125
- shared_up: bfloat16 [2560, 3072], P(None, 'mp'), may hold values from -0.125 to 0.125
- shared_down: bfloat16 [3072, 2560], P('mp'), may hold values from -0.109375 to 0.109375
- expert_gate: bfloat16 [64, 2560, 1536], P('dp', None, 'mp'), may hold values from -0.125 to 0.125
- expert_up: bfloat16 [64, 2560, 1536], P('dp', None, 'mp'), may hold values from -0.125 to 0.125
- expert_down: bfloat16 [64, 1536, 2560], P('dp', 'mp'), may hold values from -0.15625 to 0.15625
- adapter_in: bfloat16 [64, 3072, 16], P('dp', 'mp'), may hold values from -0.109375 to 0.109375
- adapter_out: bfloat16 [64, 16, 2560], P('dp'), may hold values from -1.5 to 1.5
- active: int32 [16], replicated, may hold values from 0 to 63, as said below
- lengths: int32 [64], replicated, may hold values from 1 to 1024, 4096 in all
- request_adapter: int32 [64], replicated, may hold values from 0 to 15
- routes: int32 [4096, 6], P('dp'), may hold values from 0 to 63, all different within a row; in each aligned block of 128 rows (0 to 127, 128 to 255, ...) at most 16 rows name the same one
- route_weights: float32 [4096, 6], P('dp'), may hold values from 0.05 to 0.35
Outputs:
- layer_out: bfloat16 [4096, 2560], P('dp', 'mp')
Inputs may be any that keep to these rules, and one draw needn't show every extreme that they name: `active`: the entries are distinct. `routes`: within the 128 rows of one index of dp no expert is named more than 16 times, and that many is reached; a row names distinct experts.
All inputs are finite; a program needn't handle non-finite values.
Results may differ from a plain program's by a relative error of at most 0.015.
Values may be sent and summed in bfloat16 or wider, within the bound.
No kernel may reach another device: no remote copies, remote signals or barrier semaphores. Data moves between devices by JAX's collectives and lax.ppermute only.
A program may use at most 128 MiB of HBM per device.

v0:
```python
import jax
import jax.numpy as jnp
from jax import lax
from jax.sharding import PartitionSpec as P


def experts_apply(slots_in, expert_gate, expert_up, expert_down):
    gate_val = jnp.einsum(
        "sjcd,jdf->sjcf", slots_in, expert_gate, preferred_element_type=jnp.float32
    )
    up_val = jnp.einsum("sjcd,jdf->sjcf", slots_in, expert_up, preferred_element_type=jnp.float32)
    inner = (jax.nn.silu(gate_val) * up_val).astype(jnp.bfloat16)
    return jnp.einsum("sjcf,jfd->sjcd", inner, expert_down, preferred_element_type=jnp.float32)


def body(
    hidden,
    norm_gain,
    shared_gate,
    shared_up,
    shared_down,
    expert_gate,
    expert_up,
    expert_down,
    adapter_in,
    adapter_out,
    active,
    lengths,
    request_adapter,
    routes,
    route_weights,
):
    tok_rows = routes.shape[0]
    top_count = routes.shape[1]
    dp_count = lax.axis_size("dp")
    mp_count = lax.axis_size("mp")
    dp_index = lax.axis_index("dp")
    mp_index = lax.axis_index("mp")
    local_experts = expert_gate.shape[0]
    total_experts = local_experts * dp_count
    capacity = mp_count * max(1, tok_rows * top_count * 4 // (total_experts * mp_count * 3))
    col_width = hidden.shape[1]
    col_start = mp_index * col_width
    active_count = active.shape[0]
    rank_width = adapter_in.shape[2]
    local_adapters = adapter_in.shape[0]
    owned_ids = dp_index * local_adapters + jnp.arange(local_adapters, dtype=jnp.int32)
    selector = (active[:, None] == owned_ids[None, :]).astype(jnp.bfloat16)
    out_cols = lax.dynamic_slice_in_dim(adapter_out, col_start, col_width, axis=2)
    picked_in = jnp.einsum(
        "ji,isr->jsr", selector, adapter_in, preferred_element_type=jnp.float32
    ).astype(jnp.bfloat16)
    picked_out = jnp.einsum(
        "ji,ird->jrd", selector, out_cols, preferred_element_type=jnp.float32
    ).astype(jnp.bfloat16)
    picked_in, picked_out = lax.psum((picked_in, picked_out), "dp")
    gathered = lax.all_gather(hidden, "mp", axis=1, tiled=True)
    values = gathered.astype(jnp.float32)
    factor = lax.rsqrt(jnp.mean(values * values, axis=-1, keepdims=True) + 1e-06)
    normed = (values * factor * norm_gain.astype(jnp.float32)).astype(jnp.bfloat16)
    width = normed.shape[1]
    shared_lin = jnp.dot(normed, shared_gate, preferred_element_type=jnp.float32)
    shared_pre = jnp.dot(normed, shared_up, preferred_element_type=jnp.float32)
    shared_act = (jax.nn.silu(shared_lin) * shared_pre).astype(jnp.bfloat16)
    request_end = jnp.cumsum(lengths)
    positions = dp_index * tok_rows + jnp.arange(tok_rows, dtype=jnp.int32)
    request_of = jnp.sum((request_end[None, :] <= positions[:, None]).astype(jnp.int32), axis=1)
    request_hot = (
        request_of[:, None] == jnp.arange(lengths.shape[0], dtype=jnp.int32)[None, :]
    ).astype(jnp.int32)
    slot_of = jnp.sum(request_hot * request_adapter[None, :], axis=1)
    chosen = (slot_of[:, None] == jnp.arange(active_count, dtype=jnp.int32)[None, :]).astype(
        jnp.float32
    )
    in_matrix = jnp.transpose(picked_in, (1, 0, 2)).reshape(
        shared_act.shape[1], active_count * rank_width
    )
    lowrank = jnp.dot(shared_act, in_matrix, preferred_element_type=jnp.float32)
    lowrank_sel = jnp.sum(
        lowrank.reshape(tok_rows, active_count, rank_width) * chosen[:, :, None], axis=1
    )
    lowrank_sel = lax.psum(lowrank_sel, "mp")
    lowrank = (chosen[:, :, None] * lowrank_sel[:, None, :]).reshape(
        tok_rows, active_count * rank_width
    )
    adapted = jnp.dot(
        lowrank,
        picked_out.reshape(active_count * rank_width, col_width).astype(jnp.float32),
        precision=lax.Precision.HIGHEST,
    )
    flat_routes = routes.reshape(-1)
    expert_hot = (
        flat_routes[:, None] == jnp.arange(total_experts, dtype=jnp.int32)[None, :]
    ).astype(jnp.int32)
    earlier = jnp.cumsum(expert_hot, axis=0) - expert_hot
    position = jnp.sum(earlier * expert_hot, axis=1)
    slot_index = (flat_routes * capacity + position).reshape(tok_rows, top_count)
    slot_count = total_experts * capacity
    slot_hit = slot_index[:, :, None] == jnp.arange(slot_count, dtype=jnp.int32)[None, None, :]
    dispatch = jnp.any(slot_hit, axis=1).astype(jnp.bfloat16)
    send_rows = jnp.einsum(
        "ts,td->sd", dispatch, normed, preferred_element_type=jnp.float32
    ).astype(jnp.bfloat16)
    send_rows = send_rows.reshape(dp_count, local_experts, capacity, width)
    returned = lax.all_to_all(
        experts_apply(
            lax.all_to_all(send_rows, "dp", split_axis=0, concat_axis=0, tiled=True),
            expert_gate,
            expert_up,
            expert_down,
        ).astype(jnp.bfloat16),
        "dp",
        split_axis=0,
        concat_axis=0,
        tiled=True,
    )
    returned = returned.reshape(slot_count, width)
    combine = jnp.sum(jnp.where(slot_hit, route_weights[:, :, None], 0.0), axis=1)
    combine_hi = combine.astype(jnp.bfloat16)
    combine_lo = (combine - combine_hi.astype(jnp.float32)).astype(jnp.bfloat16)
    routed = jnp.dot(combine_hi, returned, preferred_element_type=jnp.float32) + jnp.dot(
        combine_lo, returned, preferred_element_type=jnp.float32
    )
    partial_out = jnp.dot(shared_act, shared_down, preferred_element_type=jnp.float32) + routed
    own_cols = lax.dynamic_slice_in_dim(partial_out, col_start, col_width, axis=1) + adapted
    partial_out = lax.dynamic_update_slice_in_dim(partial_out, own_cols, col_start, axis=1)
    return lax.psum_scatter(partial_out.astype(jnp.bfloat16), "mp", scatter_dimension=1, tiled=True)


def solution(mesh):
    in_specs = (
        P("dp", "mp"),
        P(),
        P(None, "mp"),
        P(None, "mp"),
        P("mp", None),
        P("dp", None, "mp"),
        P("dp", None, "mp"),
        P("dp", "mp", None),
        P("dp", "mp", None),
        P("dp", None, None),
        P(),
        P(),
        P(),
        P("dp", None),
        P("dp", None),
    )
    out_specs = P("dp", "mp")
    return jax.shard_map(body, mesh=mesh, in_specs=in_specs, out_specs=out_specs, check_vma=False)
```

profile of v0, /device:TPU:0, one launch (start us, length us, event | category | flops | bytes accessed | tf_op | source)
XLA Modules:
  0.0 315.9 jit_solution(4285871344129331172)
XLA Ops:
  6.5 0.8 copy.60
  7.4 0.1 eq.85
  7.5 0.1 eq.81
  7.7 1.8 reduce-window.18
  9.5 0.3 slice_reduce_fusion
  9.8 0.1 fusion.34
  9.9 0.1 reduce_sum.58
  10.1 0.1 copy.63
  10.1 0.7 multiply_add_fusion
  10.8 0.5 fusion.9
  11.3 14.9 %all_gather.3 = bf16[128,2560]{1,0:T(8,128)(2,1)S(1)} all-gather(bf16[128,640]{1,0:T(8,128)(2,1)} %param.15), channel_id=1, replica_groups=mesh['dp'=32,'mp'=4] {'mp'}, dimensions={1}, use_global_device_ids=true | all-gather | bytes 819200 | tf_op jit(solution)/shard_map/all_gather | solution.py:57
  26.2 0.2 fusion.22
  26.5 0.7 convert_element_type.64
  27.2 1.6 convolution_convert_fusion.1
  28.8 0.0 copy-start.8
  28.8 69.5 %all_to_all.10 = bf16[32,2,16,2560]{3,2,1,0:T(8,128)(2,1)S(1)} all-to-all(bf16[32,2,16,2560]{3,2,1,0:T(8,128)(2,1)S(1)} %bitcast.98), channel_id=1, replica_groups=mesh['dp'=32,'mp'=4] {'dp'}, dimensions={0} | all-to-all | bytes 10485760 | tf_op jit(solution)/shard_map/all_to_all | solution.py:107
  98.3 2.3 copy-done.1
  100.6 2.9 fusion.3
  103.5 12.8 %fusion = bf16[32,2,16,2560]{3,2,0,1:T(8,128)(2,1)} fusion(bf16[2,384,2560]{2,1,0:T(8,128)(2,1)} %param.22, f32[2,32,16,384]{3,2,1,0:T(8,128)S(1)} %fusion.3, bf16[2,2560,384]{2,1,0:T(8,128)(2,1)} %param.21, bf16[32,2,16,2560]{3,2,1,0:T(8,128)(2,1)} %copy-done.1), kind=kOutput, calls=%fused_computation.2 | convolution fusion | flops 4031512576 | bytes 19922944 | tf_op jit(solution)/shard_map/sjcf,jfd->sjcd/dot_general | solution.py:13
  116.3 5.3 %copy.66 = bf16[32,2,16,2560]{3,2,1,0:T(8,128)(2,1)} copy(bf16[32,2,16,2560]{3,2,0,1:T(8,128)(2,1)} %fusion) | data formatting | bytes 10485760 | tf_op jit(solution)/shard_map/convert_element_type | solution.py:111
  121.5 5.0 %all-to-all-start.1 = ((bf16[32,2,16,2560]{3,2,1,0:T(8,128)(2,1)}), bf16[32,2,16,2560]{3,2,1,0:T(8,128)(2,1)}, u32[]{:S(2)}, u32[]{:S(2)}) async-start(bf16[32,2,16,2560]{3,2,1,0:T(8,128)(2,1)} %copy.66), calls=%async_computation.1 | async-start | bytes 10485760 | tf_op jit(solution)/shard_map/all_to_all | solution.py:105
  126.6 0.0 all-reduce.3.cloned.1.call-start
  126.6 0.4 fusion.25
  127.1 0.9 copy.95
  128.0 1.1 convolution_convert_fusion.3
  129.1 0.0 all-reduce.3.cloned.1.call-update
  129.1 0.2 reduce-scatter.4.cloned.1.call-start
  129.4 0.1 copy.67
  129.5 0.1 reduce-window.20
  129.5 0.1 reduce.1
  129.7 0.1 convert_reduce_fusion
  129.8 0.1 select_reduce_fusion.1
  129.9 0.4 select_reduce_fusion
  130.3 3.2 fusion.57
  133.5 0.8 fusion.26
  134.3 1.3 copy-done.2
  135.6 0.7 fusion.59
  136.3 131.0 %all-reduce.3.cloned.1.call-done = (bf16[16,16,640]{2,0,1:T(8,128)(2,1)}, bf16[16,16,768]{2,1,0:T(8,128)(2,1)}) async-done(((bf16[16,16,640]{2,0,1:T(8,128)(2,1)}, bf16[16,16,768]{2,1,0:T(8,128)(2,1)}), (bf16[16,16,640]{2,0,1:T(8,128)(2,1)}, bf16[16,16,768]{2,1,0:T(8,128)(2,1)})) %all-reduce.3.cloned.1.call-update) | async-done | bytes 720912 | tf_op jit(solution)/shard_map/psum | solution.py:56
  267.3 1.3 fusion.29
  268.6 10.8 %psum.22 = f32[128,16]{0,1:T(8,128)S(1)} all-reduce(f32[128,16]{0,1:T(8,128)S(1)} %fusion.29), channel_id=1, replica_groups=mesh['dp'=32,'mp'=4] {'mp'}, use_global_device_ids=true, to_apply=%region_11.12 | all-reduce | flops 2048 | bytes 16384 | tf_op jit(solution)/shard_map/psum | solution.py:82
  279.4 3.3 %fusion.39 = f32[128,2560]{1,0:T(8,128)S(1)} fusion(bf16[1024,2560]{1,0:T(8,128)(2,1)} %bitcast.11, f32[128,1024]{1,0:T(8,128)S(1)} %select_reduce_fusion), kind=kOutput, calls=%fused_computation.53 | convolution fusion | flops 671219712 | bytes 7077888 | tf_op jit(solution)/shard_map/dot_general | solution.py:121
  282.7 3.5 %fusion.8 = f32[128,2560]{1,0:T(8,128)S(1)} fusion(f32[128,2560]{1,0:T(8,128)S(1)} %fusion.59, f32[128,2560]{1,0:T(8,128)S(1)} %fusion.39, bf16[1024,2560]{1,0:T(8,128)(2,1)} %bitcast.11, f32[128,1024]{1,0:T(8,128)S(1)} %select_reduce_fusion), kind=kOutput, calls=%fused_computation.11 | convolution fusion | flops 672268288 | bytes 9699328 | tf_op jit(solution)/shard_map/dot_general | solution.py:121
  286.2 0.4 fusion.28
  286.6 0.1 convert_element_type.80
  286.7 1.1 copy.75
  287.8 0.0 reduce-scatter.4.cloned.1.call-update
  287.8 19.6 %reduce-scatter.4.cloned.1.call-done = bf16[640,128]{1,0:T(8,128)(2,1)} async-done(((bf16[2560,128]{1,0:T(8,128)(2,1)}), bf16[640,128]{1,0:T(8,128)(2,1)}) %reduce-scatter.4.cloned.1.call-update) | async-done | bytes 163856
  307.4 1.7 copy.76
  (27 shorter events, 0.1 us)
Async XLA Ops:
  6.5 121.4 %copy-start = (bf16[2,16,2560]{2,1,0:T(8,128)(2,1)S(1)}, bf16[2,16,2560]{2,1,0:T(8,128)(2,1)}, u32[]{:S(2)}) copy-start(bf16[2,16,2560]{2,1,0:T(8,128)(2,1)} %param.24) | copy-start | bytes 491524
  28.8 71.8 %copy-start.8 = (bf16[2,2560,384]{2,1,0:T(8,128)(2,1)S(1)}, bf16[2,2560,384]{2,1,0:T(8,128)(2,1)}, u32[]{:S(2)}) copy-start(bf16[2,2560,384]{2,1,0:T(8,128)(2,1)} %param.20) | copy-start | bytes 11796484
  98.3 2.3 copy-start.1
  121.5 5.1 %copy-start.4 = (bf16[2,768,16]{1,2,0:T(8,128)(2,1)S(1)}, bf16[2,768,16]{1,2,0:T(8,128)(2,1)}, u32[]{:S(2)}) copy-start(bf16[2,768,16]{1,2,0:T(8,128)(2,1)} %param.23) | copy-start | bytes 147460
  121.5 5.1 %copy-start.6 = (s32[16]{0:T(128)S(1)}, s32[16]{0:T(128)}, u32[]{:S(2)}) copy-start(s32[16]{0:T(128)} %param.25) | copy-start | bytes 196
  121.5 7.8 %copy-start.7 = (s32[64]{0:T(128)S(1)}, s32[64]{0:T(128)}, u32[]{:S(2)}) copy-start(s32[64]{0:T(128)} %param.26) | copy-start | bytes 772
  121.5 8.2 %copy-start.10 = (s32[64]{0:T(128)S(1)}, s32[64]{0:T(128)}, u32[]{:S(2)}) copy-start(s32[64]{0:T(128)} %param.27) | copy-start | bytes 772
  121.5 8.3 %copy-start.5 = (f32[128,6]{0,1:T(8,128)S(1)}, f32[128,6]{0,1:T(8,128)}, u32[]{:S(2)}) copy-start(f32[128,6]{0,1:T(8,128)} %param.29) | copy-start | bytes 9220
  121.5 157.8 %all-to-all-start.1 = ((bf16[32,2,16,2560]{3,2,1,0:T(8,128)(2,1)}), bf16[32,2,16,2560]{3,2,1,0:T(8,128)(2,1)}, u32[]{:S(2)}, u32[]{:S(2)}) async-start(bf16[32,2,16,2560]{3,2,1,0:T(8,128)(2,1)} %copy.66), calls=%async_computation.1 | async-start | bytes 10485760 | tf_op jit(solution)/shard_map/all_to_all | solution.py:105
  126.6 140.7 %all-reduce.3.cloned.1.call-start = ((), (), s32[]{:S(2)}) async-start(), calls=%async_computation.4 | async-start | bytes 1441792 | tf_op jit(solution)/shard_map/psum | solution.py:56
  129.1 178.2 %reduce-scatter.4.cloned.1.call-start = ((), (), s32[]{:S(2)}) async-start(), calls=%async_computation.3 | async-start | bytes 819200
  129.7 3.8 %copy-start.9 = (bf16[2560,768]{1,0:T(8,128)(2,1)S(1)}, bf16[2560,768]{1,0:T(8,128)(2,1)}, u32[]{:S(2)}) copy-start(bf16[2560,768]{1,0:T(8,128)(2,1)} %param.18) | copy-start | bytes 11796484
  133.5 2.1 copy-start.2
  282.7 3.5 %copy-start.3 = (bf16[16,16,640]{2,0,1:T(8,128)(2,1)S(1)}, bf16[16,16,640]{2,0,1:T(8,128)(2,1)}, u32[]{:S(2)}) copy-start(bf16[16,16,640]{2,0,1:T(8,128)(2,1)} %get-tuple-element.5) | copy-start | bytes 983044
Sparse Core Ops, SparseCore 0:
  130.8 136.4 all-reduce.2
  287.9 19.4 reduce-scatter.3
where the time goes:
time: 316 us
  waiting for transfers between devices  151 us (48%)
  blocking collectives  95.2 us (30%)
  matrix products  31.9 us (10%)
  local copies, waits for them, and re-layouts  14.3 us (5%)
  between operations  13.7 us (4%)
  starting transfers between devices  5.27 us (2%)
  other arithmetic  4.99 us (2%)
    psum x1, waiting for transfers between devices, body(): picked_in, picked_out = lax.psum((picked_in, picked_out), 'dp')  131 us
    all_to_all x1, blocking collectives, body(): lax.all_to_all(send_rows, 'dp', split_axis=0, concat_axis=0, tiled=True)  69.5 us
    unnamed x3, waiting for transfers between devices  19.6 us
    all_gather x1, blocking collectives, body(): gathered = lax.all_gather(hidden, 'mp', axis=1, tiled=True)  14.9 us
    dot_general x1, matrix products, experts_apply(): jnp.einsum('sjcf,jfd->sjcd', inner, expert_down, preferred_element_type=j...  12.8 us
    psum x1, blocking collectives, body(): lowrank_sel = lax.psum(lowrank_sel, 'mp')  10.8 us
    unnamed x25, local copies, waits for them, and re-layouts  7.3 us
  transfers between devices with their start and end apart: 3, of which 2 were waited for; matrix products, arithmetic and copies ran while one was open for 3% of the time, Pallas kernels for 0%

commit v1 on v0

--- a/solution.py
+++ b/solution.py
@@ -79,7 +79,11 @@
     lowrank_sel = jnp.sum(
         lowrank.reshape(tok_rows, active_count, rank_width) * chosen[:, :, None], axis=1
     )
-    lowrank_sel = lax.psum(lowrank_sel, "mp")
+    lowrank_sel = lowrank_sel
+    for hop in (1, 2):
+        lowrank_sel = lowrank_sel + lax.ppermute(
+            lowrank_sel, "mp", [(dev, dev ^ hop) for dev in range(4)]
+        )
     lowrank = (chosen[:, :, None] * lowrank_sel[:, None, :]).reshape(
         tok_rows, active_count * rank_width
     )

time: 316 us -> 319 us (level)
  blocking collectives: 95.2 us -> 84.4 us
  waiting for transfers between devices: 151 us -> 157 us
  starting transfers between devices: 5.27 us -> 9.84 us
  matrix products: 31.9 us -> 35.4 us
    psum x1 -> x0, blocking collectives: 10.8 us -> none  [body(): lowrank_sel = lax.psum(lowrank_sel, 'mp')]
    ppermute x0 -> x2, starting transfers between devices: none -> 4.75 us  [body(): lax.ppermute(lowrank_sel, 'mp', [(dev, dev ^ hop) for dev in range(4)])]
    unnamed x25 -> x23, local copies, waits for them, and re-layouts: 7.3 us -> 6.06 us
  transfers between devices with their start and end apart: 3 -> 5, of which waited for: 2 -> 3; matrix products, arithmetic and copies ran while one was open for 3% -> 4% of each run, Pallas kernels for 0% -> 0%
where the time goes in v1:
time: 319 us
  waiting for transfers between devices  157 us (49%)
  blocking collectives  84.4 us (26%)
  matrix products  35.4 us (11%)
  between operations  13.7 us (4%)
  local copies, waits for them, and re-layouts  13 us (4%)
  starting transfers between devices  9.84 us (3%)
  other arithmetic  4.99 us (2%)
    psum x1, waiting for transfers between devices, body(): picked_in, picked_out = lax.psum((picked_in, picked_out), 'dp')  134 us
    all_to_all x1, blocking collectives, body(): lax.all_to_all(send_rows, 'dp', split_axis=0, concat_axis=0, tiled=True)  69.5 us
    unnamed x3, waiting for transfers between devices  21.6 us
    all_gather x1, blocking collectives, body(): gathered = lax.all_gather(hidden, 'mp', axis=1, tiled=True)  14.9 us
    dot_general x1, matrix products, experts_apply(): jnp.einsum('sjcf,jfd->sjcd', inner, expert_down, preferred_element_type=j...  13.2 us
  transfers between devices with their start and end apart: 5, of which 3 were waited for; matrix products, arithmetic and copies ran while one was open for 4% of the time, Pallas kernels for 0%

profile of v1, /device:TPU:0, one launch (start us, length us, event | category | flops | bytes accessed | tf_op | source)
XLA Modules:
  0.0 318.6 jit_solution(10573686482799431132)
XLA Ops:
  6.5 0.8 copy.60
  7.4 0.1 eq.85
  7.5 0.1 eq.81
  7.7 1.8 reduce-window.18
  9.5 0.3 slice_reduce_fusion
  9.8 0.1 fusion.34
  9.9 0.1 reduce_sum.58
  10.1 0.1 copy.63
  10.1 0.7 multiply_add_fusion
  10.8 0.5 fusion.9
  11.3 14.9 %all_gather.3 = bf16[128,2560]{1,0:T(8,128)(2,1)S(1)} all-gather(bf16[128,640]{1,0:T(8,128)(2,1)} %param.15), channel_id=1, replica_groups=mesh['dp'=32,'mp'=4] {'mp'}, dimensions={1}, use_global_device_ids=true | all-gather | bytes 819200 | tf_op jit(solution)/shard_map/all_gather | solution.py:57
  26.2 0.2 fusion.22
  26.5 0.7 convert_element_type.64
  27.2 1.6 convolution_convert_fusion.1
  28.8 69.5 %all_to_all.10 = bf16[32,2,16,2560]{3,2,1,0:T(8,128)(2,1)S(1)} all-to-all(bf16[32,2,16,2560]{3,2,1,0:T(8,128)(2,1)S(1)} %bitcast.98), channel_id=1, replica_groups=mesh['dp'=32,'mp'=4] {'dp'}, dimensions={0} | all-to-all | bytes 10485760 | tf_op jit(solution)/shard_map/all_to_all | solution.py:111
  98.3 2.3 copy-done.1
  100.6 4.0 %fusion.3 = f32[2,32,16,384]{3,2,1,0:T(8,128)} fusion(bf16[32,2,16,2560]{3,2,1,0:T(8,128)(2,1)S(1)} %all_to_all.10, bf16[2,2560,384]{2,1,0:T(8,128)(2,1)S(1)} %copy-done.7), kind=kOutput, calls=%fused_computation.5 | convolution fusion | flops 2013265920 | bytes 10747904 | tf_op jit(solution)/shard_map/sjcd,jdf->sjcf/dot_general | solution.py:8
  104.6 13.2 %fusion = bf16[32,2,16,2560]{3,2,0,1:T(8,128)(2,1)} fusion(bf16[2,384,2560]{2,1,0:T(8,128)(2,1)} %param.22, f32[2,32,16,384]{3,2,1,0:T(8,128)} %fusion.3, bf16[2,2560,384]{2,1,0:T(8,128)(2,1)} %param.21, bf16[32,2,16,2560]{3,2,1,0:T(8,128)(2,1)} %copy-done.1), kind=kOutput, calls=%fused_computation.2 | convolution fusion | flops 4031512576 | bytes 19922944 | tf_op jit(solution)/shard_map/sjcf,jfd->sjcd/dot_general | solution.py:13
  117.8 5.3 %copy.66 = bf16[32,2,16,2560]{3,2,1,0:T(8,128)(2,1)} copy(bf16[32,2,16,2560]{3,2,0,1:T(8,128)(2,1)} %fusion) | data formatting | bytes 10485760 | tf_op jit(solution)/shard_map/convert_element_type | solution.py:115
  123.1 5.0 %all-to-all-start.1 = ((bf16[32,2,16,2560]{3,2,1,0:T(8,128)(2,1)}), bf16[32,2,16,2560]{3,2,1,0:T(8,128)(2,1)}, u32[]{:S(2)}, u32[]{:S(2)}) async-start(bf16[32,2,16,2560]{3,2,1,0:T(8,128)(2,1)} %copy.66), calls=%async_computation.1 | async-start | bytes 10485760 | tf_op jit(solution)/shard_map/all_to_all | solution.py:109
  128.1 0.0 all-reduce.3.cloned.1.call-start
  128.2 0.4 fusion.25
  128.7 0.9 copy.95
  129.5 1.1 convolution_convert_fusion.3
  130.7 0.0 all-reduce.3.cloned.1.call-update
  130.7 0.0 reduce-scatter.4.cloned.1.call-start
  130.8 0.1 copy.67
  130.9 0.1 reduce-window.20
  131.0 0.1 reduce.1
  131.1 0.1 convert_reduce_fusion
  131.2 0.1 select_reduce_fusion.1
  131.3 3.0 fusion.57
  134.3 0.1 copy-done.8
  134.4 0.8 fusion.26
  135.2 133.7 %all-reduce.3.cloned.1.call-done = (bf16[16,16,640]{2,0,1:T(8,128)(2,1)}, bf16[16,16,768]{2,1,0:T(8,128)(2,1)}) async-done(((bf16[16,16,640]{2,0,1:T(8,128)(2,1)}, bf16[16,16,768]{2,1,0:T(8,128)(2,1)}), (bf16[16,16,640]{2,0,1:T(8,128)(2,1)}, bf16[16,16,768]{2,1,0:T(8,128)(2,1)})) %all-reduce.3.cloned.1.call-update) | async-done | bytes 720912 | tf_op jit(solution)/shard_map/psum | solution.py:56
  268.9 1.3 fusion.29
  270.1 1.8 collective-permute-start
  271.9 2.8 fusion.59
  274.8 2.9 collective-permute-start.1
  277.7 0.4 select_reduce_fusion
  278.1 1.9 collective-permute-done.1
  280.0 3.3 %fusion.39 = f32[128,2560]{1,0:T(8,128)S(1)} fusion(bf16[1024,2560]{1,0:T(8,128)(2,1)} %bitcast.11, f32[128,1024]{1,0:T(8,128)S(1)} %select_reduce_fusion), kind=kOutput, calls=%fused_computation.53 | convolution fusion | flops 671219712 | bytes 7077888 | tf_op jit(solution)/shard_map/dot_general | solution.py:125
  283.4 3.5 %fusion.8 = f32[128,2560]{1,0:T(8,128)S(1)} fusion(f32[128,2560]{1,0:T(8,128)S(1)} %fusion.59, f32[128,2560]{1,0:T(8,128)S(1)} %fusion.39, bf16[1024,2560]{1,0:T(8,128)(2,1)} %bitcast.11, f32[128,1024]{1,0:T(8,128)S(1)} %select_reduce_fusion), kind=kOutput, calls=%fused_computation.11 | convolution fusion | flops 672268288 | bytes 9699328 | tf_op jit(solution)/shard_map/dot_general | solution.py:125
  286.9 0.4 fusion.28
  287.3 0.1 convert_element_type.80
  287.3 1.1 copy.75
  288.4 21.6 %reduce-scatter.4.cloned.1.call-done = bf16[640,128]{1,0:T(8,128)(2,1)} async-done(((bf16[2560,128]{1,0:T(8,128)(2,1)}), bf16[640,128]{1,0:T(8,128)(2,1)}) %reduce-scatter.4.cloned.1.call-update) | async-done | bytes 163856
  310.0 1.7 copy.76
  (30 shorter events, 0.1 us)
Async XLA Ops:
  6.5 123.0 %copy-start = (bf16[2,16,2560]{2,1,0:T(8,128)(2,1)S(1)}, bf16[2,16,2560]{2,1,0:T(8,128)(2,1)}, u32[]{:S(2)}) copy-start(bf16[2,16,2560]{2,1,0:T(8,128)(2,1)} %param.24) | copy-start | bytes 491524
  28.8 71.8 %copy-start.7 = (bf16[2,2560,384]{2,1,0:T(8,128)(2,1)S(1)}, bf16[2,2560,384]{2,1,0:T(8,128)(2,1)}, u32[]{:S(2)}) copy-start(bf16[2,2560,384]{2,1,0:T(8,128)(2,1)} %param.20) | copy-start | bytes 11796484
  98.3 2.3 copy-start.1
  123.1 5.1 %copy-start.3 = (bf16[2,768,16]{1,2,0:T(8,128)(2,1)S(1)}, bf16[2,768,16]{1,2,0:T(8,128)(2,1)}, u32[]{:S(2)}) copy-start(bf16[2,768,16]{1,2,0:T(8,128)(2,1)} %param.23) | copy-start | bytes 147460
  123.1 5.1 %copy-start.5 = (s32[16]{0:T(128)S(1)}, s32[16]{0:T(128)}, u32[]{:S(2)}) copy-start(s32[16]{0:T(128)} %param.25) | copy-start | bytes 196
  123.1 7.6 %copy-start.6 = (s32[64]{0:T(128)S(1)}, s32[64]{0:T(128)}, u32[]{:S(2)}) copy-start(s32[64]{0:T(128)} %param.26) | copy-start | bytes 772
  123.1 8.1 %copy-start.9 = (s32[64]{0:T(128)S(1)}, s32[64]{0:T(128)}, u32[]{:S(2)}) copy-start(s32[64]{0:T(128)} %param.27) | copy-start | bytes 772
  123.1 156.9 %all-to-all-start.1 = ((bf16[32,2,16,2560]{3,2,1,0:T(8,128)(2,1)}), bf16[32,2,16,2560]{3,2,1,0:T(8,128)(2,1)}, u32[]{:S(2)}, u32[]{:S(2)}) async-start(bf16[32,2,16,2560]{3,2,1,0:T(8,128)(2,1)} %copy.66), calls=%async_computation.1 | async-start | bytes 10485760 | tf_op jit(solution)/shard_map/all_to_all | solution.py:109
  128.1 140.7 %all-reduce.3.cloned.1.call-start = ((), (), s32[]{:S(2)}) async-start(), calls=%async_computation.4 | async-start | bytes 1441792 | tf_op jit(solution)/shard_map/psum | solution.py:56
  130.7 179.4 %reduce-scatter.4.cloned.1.call-start = ((), (), s32[]{:S(2)}) async-start(), calls=%async_computation.3 | async-start | bytes 819200
  131.1 3.3 %copy-start.8 = (bf16[2560,768]{1,0:T(8,128)(2,1)S(1)}, bf16[2560,768]{1,0:T(8,128)(2,1)}, u32[]{:S(2)}) copy-start(bf16[2560,768]{1,0:T(8,128)(2,1)} %param.18) | copy-start | bytes 11796484
  135.1 142.6 %copy-start.4 = (f32[128,6]{0,1:T(8,128)S(1)}, f32[128,6]{0,1:T(8,128)}, u32[]{:S(2)}) copy-start(f32[128,6]{0,1:T(8,128)} %param.29) | copy-start | bytes 9220
  270.1 4.6 %collective-permute-start = (f32[128,16]{0,1:T(8,128)S(1)}, f32[128,16]{0,1:T(8,128)S(1)}, u32[]{:S(2)}, u32[]{:S(2)}) collective-permute-start(f32[128,16]{0,1:T(8,128)S(1)} %fusion.29), channel_id=1, source_target_pairs={{0,1},{1,0},{2,3},{3,2},{4,5},{5,4},{6,7},{7,6},{8,9},{9,8},{10,11... | collective-permute-start | bytes 24584 | tf_op jit(solution)/shard_map/ppermute | solution.py:84
  274.8 5.2 %collective-permute-start.1 = (f32[128,16]{0,1:T(8,128)S(1)}, f32[128,16]{0,1:T(8,128)S(1)}, u32[]{:S(2)}, u32[]{:S(2)}) collective-permute-start(f32[128,16]{0,1:T(8,128)S(1)} %add.82), channel_id=1, source_target_pairs={{0,2},{1,3},{2,0},{3,1},{4,6},{5,7},{6,4},{7,5},{8,10},{9,11},{10,... | collective-permute-start | bytes 24584 | tf_op jit(solution)/shard_map/ppermute | solution.py:84
  283.4 3.5 %copy-start.2 = (bf16[16,16,640]{2,0,1:T(8,128)(2,1)S(1)}, bf16[16,16,640]{2,0,1:T(8,128)(2,1)}, u32[]{:S(2)}) copy-start(bf16[16,16,640]{2,0,1:T(8,128)(2,1)} %get-tuple-element.5) | copy-start | bytes 983044
Sparse Core Ops, SparseCore 0:
  132.3 136.4 all-reduce.2
  288.6 21.4 reduce-scatter.3
